TPU v7x, 32 devices: a whole 2x2x4 slice. The times are simulated.
32 devices in a mesh: req: 8 (over z, y), tp: 4 (over x, core).
Axes of the slice: x: 2, y: 2, z: 4, core: 2. Of those that a mesh axis runs over, the one named last changes fastest.
Arguments:
- hidden: bfloat16 [4096, 2048], P('req', 'tp'), may hold values from -6 to 6
- queries: bfloat16 [4096, 2048], P('req', 'tp'), may hold values from -4 to 4
- new_keys: bfloat16 [4096, 512], P('req'), may hold values from -4 to 4
- new_values: bfloat16 [4096, 512], P('req'), may hold values from -6 to 6
- cache_keys: bfloat16 [384, 64, 512], P('req'), may hold values from -6 to 6
- cache_values: bfloat16 [384, 64, 512], P('req'), may hold values from -6 to 6
- out_weight: bfloat16 [2048, 2048], P('tp'), may hold values from -0.125 to 0.125
- attn_gain: bfloat16 [2048], P('tp'), may hold values from 0.099609375 to 1.8984375
- ple_input: bfloat16 [4096, 256], P('req'), may hold values from -6 to 6
- ple_gate_weight: bfloat16 [2048, 256], P('tp'), may hold values from -0.125 to 0.125
- ple_proj_weight: bfloat16 [256, 2048], P(None, 'tp'), may hold values from -0.375 to 0.375
- ple_gain: bfloat16 [2048], P('tp'), may hold values from 0.099609375 to 1.8984375
- page_holder: int32 [384, 1], P('req'), may hold values from 0 to 7; in each aligned block of 48 rows (0 to 47, 48 to 95, ...) at most 6 rows name the same one
- page_slot: int32 [384, 1], P('req'), may hold values from 0 to 47
- page_counts: int32 [8, 8], P('req'), may hold values from 1 to 12, 48 in all within a row
- last_fill: int32 [8, 8], P('req'), may hold values from 1 to 64
- row_counts: int32 [8, 8], P('req'), may hold values from 1 to 256, 512 in all within a row
Outputs:
- layer_out: bfloat16 [4096, 2048], P('req', 'tp')
Inputs may be any that keep to these rules, and one draw needn't show every extreme that they name: `page_holder`: within the 48 page references of one device's requests (aligned blocks), no req index is named more than 6 times; in some block one is named exactly 6 times. `page_counts`: the 8 counts of one device sum to 48; some count equals 12. `row_counts`: the 8 counts of one device sum to 512; some count equals 256.
All inputs are finite; a program needn't handle non-finite values.
Results may differ from a plain program's by a relative error of at most 0.0061.
Values may be sent and summed in bfloat16 or wider, within the bound.
No kernel may reach another device: no remote copies, remote signals or barrier semaphores. Data moves between devices by JAX's collectives and lax.ppermute only.
A program may use at most 128 MiB of HBM per device.

v0:
```python
import math
import jax
import jax.numpy as jnp
from jax import lax
from jax.sharding import PartitionSpec as P

D = 2048
HD = 256


def slot_lookup(positions, counts):
    starts = jnp.cumsum(counts) - counts
    owning = jnp.sum((positions[:, None] >= starts[None, :]).astype(jnp.int32), axis=1) - 1
    return (owning, starts)


def table_pick(table, owning):
    onehot = owning[:, None] == jnp.arange(table.shape[0], dtype=jnp.int32)[None, :]
    return jnp.sum(jnp.where(onehot, table[None, :], 0), axis=1)


def attend_masks(counts_of_pages, fill_row, counts_of_rows, page_len, page_total, row_total):
    key_index = jnp.arange(page_total * page_len, dtype=jnp.int32)
    page_ref = key_index // page_len
    within = key_index % page_len
    page_owner, page_starts = slot_lookup(page_ref, counts_of_pages)
    context_len = (counts_of_pages - 1) * page_len + fill_row
    position = (page_ref - table_pick(page_starts, page_owner)) * page_len + within
    valid = position < table_pick(context_len, page_owner)
    row_index = jnp.arange(row_total, dtype=jnp.int32)
    row_owner = slot_lookup(row_index, counts_of_rows)[0]
    context_mask = (row_owner[:, None] == page_owner[None, :]) & valid[None, :]
    causal = (row_owner[:, None] == row_owner[None, :]) & (row_index[None, :] <= row_index[:, None])
    return jnp.concatenate([context_mask, causal], axis=1)


def shards(
    hidden,
    queries,
    new_keys,
    new_values,
    cache_keys,
    cache_values,
    out_weight,
    attn_gain,
    ple_input,
    ple_gate_weight,
    ple_proj_weight,
    ple_gain,
    page_holder,
    page_slot,
    page_counts,
    last_fill,
    row_counts,
):
    row_total = hidden.shape[0]
    page_total = cache_keys.shape[0]
    page_len = cache_keys.shape[1]
    req_count = lax.axis_size("req")
    tp_index = lax.axis_index("tp")
    local_heads = queries.shape[1] // HD
    kv_head = tp_index // 2
    capacity = max(2, page_total // req_count)
    holders = page_holder[:, 0]
    places = page_slot[:, 0]
    ref_index = jnp.arange(page_total, dtype=jnp.int32)
    earlier = (holders[:, None] == holders[None, :]) & (ref_index[:, None] > ref_index[None, :])
    ranking = jnp.sum(earlier.astype(jnp.int32), axis=1)
    matched = (holders[:, None, None] == jnp.arange(req_count, dtype=jnp.int32)[None, :, None]) & (
        ranking[:, None, None] == jnp.arange(capacity, dtype=jnp.int32)[None, None, :]
    )
    request_table = jnp.sum(jnp.where(matched, places[:, None, None] + 1, 0), axis=0) - 1
    asked = lax.all_to_all(request_table, "req", split_axis=0, concat_axis=0, tiled=True)
    wanted = jnp.maximum(asked, 0)
    head_keys = lax.dynamic_slice_in_dim(cache_keys, kv_head * HD, HD, 2)
    head_values = lax.dynamic_slice_in_dim(cache_values, kv_head * HD, HD, 2)
    stacked = jnp.concatenate([head_keys, head_values], axis=2)
    arrival_index = holders * capacity + ranking
    outgoing = stacked[wanted]
    arrived = lax.all_to_all(outgoing, "req", split_axis=0, concat_axis=0, tiled=True)
    context = arrived.reshape(req_count * capacity, page_len, 2 * HD)[arrival_index]
    context_keys = context[:, :, :HD].reshape(page_total * page_len, HD)
    context_values = context[:, :, HD:].reshape(page_total * page_len, HD)
    fresh_keys = lax.dynamic_slice_in_dim(new_keys, kv_head * HD, HD, 1)
    fresh_values = lax.dynamic_slice_in_dim(new_values, kv_head * HD, HD, 1)
    all_keys = jnp.concatenate([context_keys, fresh_keys], axis=0)
    all_values = jnp.concatenate([context_values, fresh_values], axis=0)
    masking = attend_masks(
        page_counts[0], last_fill[0], row_counts[0], page_len, page_total, row_total
    )
    query_rows = queries.reshape(row_total, local_heads, HD)
    scores = jnp.einsum("rhd,kd->hrk", query_rows, all_keys, preferred_element_type=jnp.float32) * (
        1.0 / math.sqrt(HD)
    )
    scores = jnp.where(masking[None], scores, -1e30)
    highest = jnp.max(scores, axis=-1, keepdims=True)
    expo = jnp.exp(scores - highest)
    weights = (expo / jnp.sum(expo, axis=-1, keepdims=True)).astype(jnp.bfloat16)
    attention = jnp.einsum("hrk,kd->rhd", weights, all_values, preferred_element_type=jnp.float32)
    attention = attention.astype(jnp.bfloat16).reshape(row_total, local_heads * HD)
    tp_size = lax.axis_size("tp")
    full_weight = lax.all_gather(out_weight, "tp", axis=0, tiled=True)
    full_gate_weight = lax.all_gather(ple_gate_weight, "tp", axis=0, tiled=True)
    full_proj_weight = lax.all_gather(ple_proj_weight, "tp", axis=1, tiled=True)
    full_attn_gain = lax.all_gather(attn_gain, "tp", axis=0, tiled=True)
    full_ple_gain = lax.all_gather(ple_gain, "tp", axis=0, tiled=True)
    row_hidden = lax.all_to_all(hidden, "tp", split_axis=0, concat_axis=1, tiled=True)
    row_attention = lax.all_to_all(attention, "tp", split_axis=0, concat_axis=1, tiled=True)
    part_rows = row_attention.shape[0]
    row_ple = lax.dynamic_slice_in_dim(ple_input, tp_index * part_rows, part_rows, 0)
    projected = jnp.dot(row_attention, full_weight, preferred_element_type=jnp.float32)
    squares = jnp.sum(projected * projected, axis=1)
    normed = (
        projected
        * lax.rsqrt(squares / D + 1e-06)[:, None]
        * full_attn_gain.astype(jnp.float32)[None, :]
    )
    mixed_state = (row_hidden.astype(jnp.float32) + normed).astype(jnp.bfloat16)
    gate = jnp.dot(mixed_state, full_gate_weight, preferred_element_type=jnp.float32)
    activated = (jax.nn.gelu(gate, approximate=True) * row_ple.astype(jnp.float32)).astype(
        jnp.bfloat16
    )
    lifted = jnp.dot(activated, full_proj_weight, preferred_element_type=jnp.float32)
    lift_squares = jnp.sum(lifted * lifted, axis=1)
    lift_normed = (
        lifted
        * lax.rsqrt(lift_squares / D + 1e-06)[:, None]
        * full_ple_gain.astype(jnp.float32)[None, :]
    )
    row_out = (mixed_state.astype(jnp.float32) + lift_normed).astype(jnp.bfloat16)
    return lax.all_to_all(row_out, "tp", split_axis=1, concat_axis=0, tiled=True)


def solution(mesh):
    return jax.shard_map(
        shards,
        mesh=mesh,
        in_specs=(
            P("req", "tp"),
            P("req", "tp"),
            P("req", None),
            P("req", None),
            P("req", None, None),
            P("req", None, None),
            P("tp", None),
            P("tp"),
            P("req", None),
            P("tp", None),
            P(None, "tp"),
            P("tp"),
            P("req", None),
            P("req", None),
            P("req", None),
            P("req", None),
            P("req", None),
        ),
        out_specs=P("req", "tp"),
        check_vma=False,
    )
```

profile of v0, /device:TPU:0, one launch (start us, length us, event | category | flops | bytes accessed | tf_op | source)
XLA Modules:
  0.0 189.8 jit_solution(16006355638064620231)
XLA Ops:
  6.5 0.7 all-gather.6.cloned.1.call-update
  7.3 0.9 convert_reduce_fusion.1
  8.2 0.7 add_bitcast_fusion.2
  9.7 0.7 copy.41
  10.4 7.3 %all-to-all-start.1 = ((s32[8,1,6]{2,1,0:T(1,128)}), s32[8,1,6]{2,1,0:T(1,128)S(1)}, u32[]{:S(2)}, u32[]{:S(2)}) async-start(s32[8,1,6]{2,1,0:T(1,128)} %copy.41), calls=%async_computation.1 | async-start | bytes 8192 | tf_op jit(solution)/shard_map/all_to_all | solution.py:73
  17.7 2.7 %constant_dynamic-slice_fusion.2 = (bf16[48,64,256]{2,1,0:T(8,128)(2,1)S(1)}, bf16[48,64,256]{2,1,0:T(8,128)(2,1)S(1)}) fusion(bf16[48,64,512]{2,1,0:T(8,128)(2,1)} %param.22, s32[]{:T(128)S(6)} %select_n.60, bf16[48,64,512]{2,1,0:T(8,128)(2,1)} %param.21), kind=kLoop, calls=%fused_computation.83 | loop fusion | bytes 6291460 | tf_op jit(solution)/shard_map/dynamic_slice | solution.py:76
  20.6 3.4 %all-to-all-done.1 = s32[8,1,6]{2,1,0:T(1,128)S(1)} async-done(((s32[8,1,6]{2,1,0:T(1,128)}), s32[8,1,6]{2,1,0:T(1,128)S(1)}, u32[]{:S(2)}, u32[]{:S(2)}) %all-to-all-start.1) | async-done | bytes 224 | tf_op jit(solution)/shard_map/all_to_all | solution.py:73
  24.2 2.5 %gather_fusion = bf16[48,64,512]{2,1,0:T(8,128)(2,1)} fusion(bf16[48,64,512]{2,1,0:T(8,128)(2,1)S(1)} %pad_maximum_fusion, s32[1024]{0:T(1024)S(1)} %pad_clamp_fusion.1), kind=kCustom, calls=%fused_computation | custom fusion | bytes 6291648 | tf_op jit(solution)/shard_map/gather | solution.py:79
  26.7 3.8 %all-to-all-start.2 = ((bf16[8,6,64,512]{3,2,1,0:T(8,128)(2,1)}), bf16[8,6,64,512]{3,2,1,0:T(8,128)(2,1)S(1)}, u32[]{:S(2)}, u32[]{:S(2)}) async-start(bf16[8,6,64,512]{3,2,1,0:T(8,128)(2,1)} %bitcast.73), calls=%async_computation.2 | async-start | bytes 6291456 | tf_op jit(solution)/shard_map/all_to_all | solution.py:80
  30.5 0.7 all-gather.10.cloned.1.call-update
  31.6 1.8 constant_dynamic-slice_fusion
  33.4 0.8 copy.51
  34.8 2.4 %compare_and_fusion = pred[512,3072]{0,1:T(8,128)(4,1)S(1)} fusion(s32[512]{0:T(512)S(1)} %broadcast_add_fusion.1, s32[3072]{0:T(1024)S(1)} %broadcast_add_fusion, pred[3072]{0:T(1024)(128)(4,1)S(1)} %fusion.40), kind=kLoop, calls=%fused_computation.12 | loop fusion | flops 3145728 | bytes 1590272 | tf_op jit(solution)/shard_map/and | solution.py:32
  37.2 1.7 pad_add_fusion
  38.9 61.1 %all-to-all-done.2 = bf16[8,6,64,512]{3,2,1,0:T(8,128)(2,1)S(1)} async-done(((bf16[8,6,64,512]{3,2,1,0:T(8,128)(2,1)}), bf16[8,6,64,512]{3,2,1,0:T(8,128)(2,1)S(1)}, u32[]{:S(2)}, u32[]{:S(2)}) %all-to-all-start.2) | async-done | bytes 3145760 | tf_op jit(solution)/shard_map/all_to_all | solution.py:80
  100.0 4.1 %all-to-all-start = ((bf16[4,128,512]{2,1,0:T(8,128)(2,1)}), bf16[4,128,512]{2,1,0:T(8,128)(2,1)}, u32[]{:S(2)}, u32[]{:S(2)}) async-start(bf16[4,128,512]{2,1,0:T(8,128)(2,1)} %bitcast.82), calls=%async_computation | async-start | bytes 1048576 | tf_op jit(solution)/shard_map/all_to_all | solution.py:107
  104.1 2.5 %gather_fusion.1 = bf16[48,64,512]{2,1,0:T(8,128)(2,1)} fusion(bf16[48,64,512]{2,1,0:T(8,128)(2,1)S(1)} %bitcast.72, s32[1024]{0:T(1024)S(1)} %pad_clamp_fusion), kind=kCustom, calls=%fused_computation.1 | custom fusion | bytes 6291648 | tf_op jit(solution)/shard_map/gather | solution.py:81
  106.6 2.1 %fusion.52 = (bf16[48,64,256]{2,1,0:T(8,128)(2,1)S(1)}, bf16[48,64,256]{2,1,0:T(8,128)(2,1)S(1)}) fusion(bf16[48,64,512]{2,1,0:T(8,128)(2,1)} %gather_fusion.1), kind=kLoop, calls=%fused_computation.102 | loop fusion | bytes 6291456 | tf_op jit(solution)/shard_map/slice | solution.py:83
  108.7 1.8 copy.43
  110.5 8.6 %fusion.8 = f32[3584,512,2]{1,0,2:T(8,128)} fusion(bf16[512,256]{1,0:T(8,128)(2,1)} %get-tuple-element.17, bf16[3072,256]{1,0:T(8,128)(2,1)S(1)} %bitcast.74, bf16[64,2,8,256]{3,2,1,0:T(8,128)(2,1)} %bitcast.81), kind=kOutput, calls=%fused_computation.18 | convolution fusion | flops 1882718208 | bytes 17039360 | tf_op jit(solution)/shard_map/rhd,kd->hrk/dot_general | solution.py:92
  119.1 16.0 %fusion.53 = (f32[2,512]{1,0:T(2,128)S(1)}, f32[2,512,3584]{1,2,0:T(8,128)}) fusion(f32[3584,512,2]{1,0,2:T(8,128)} %fusion.8, pred[512,3584]{0,1:T(8,128)(4,1)S(1)} %copy-done), kind=kOutput, calls=%fused_computation.103 | output fusion | flops 22023680 | bytes 31199232 | tf_op jit(solution)/shard_map/sub | solution.py:97
  135.0 7.3 %fusion.12 = bf16[512,2,256]{0,2,1:T(8,128)(2,1)S(1)} fusion(f32[2,512,3584]{1,2,0:T(8,128)} %get-tuple-element.12, f32[2,512]{1,0:T(2,128)S(1)} %get-tuple-element.11, bf16[512,256]{0,1:T(8,128)(2,1)} %copy.51, bf16[3072,256]{0,1:T(8,128)(2,1)S(1)} %copy-done.1), kind=kOutput, calls=%fused_computation.22 | convolution fusion | flops 1890320384 | bytes 17043456 | tf_op jit(solution)/shard_map/hrk,kd->rhd/dot_general | solution.py:99
  142.5 0.9 copy.46
  143.4 3.7 %all-to-all-start.3 = ((bf16[4,128,512]{1,2,0:T(8,128)(2,1)}), bf16[4,128,512]{1,2,0:T(8,128)(2,1)S(1)}, u32[]{:S(2)}, u32[]{:S(2)}) async-start(bf16[4,128,512]{1,2,0:T(8,128)(2,1)} %copy.46), calls=%async_computation.3 | async-start | bytes 1048576 | tf_op jit(solution)/shard_map/all_to_all | solution.py:108
  147.1 0.7 all-gather.8.cloned.1.call-update
  147.8 9.0 %all-gather = bf16[4,1,512]{2,1,0:T(2,128)(2,1)S(1)} all-gather(bf16[1,1,512]{2,1,0:T(2,128)(2,1)S(1)} %reshape.210), channel_id=1, replica_groups=mesh['req'=8,'tp'=4] {'tp'}, dimensions={0}, use_global_device_ids=true | all-gather | bytes 5120 | tf_op jit(solution)/shard_map/all_gather | solution.py:105
  156.8 5.2 %all-gather.1 = bf16[4,1,512]{2,1,0:T(2,128)(2,1)S(1)} all-gather(bf16[1,1,512]{2,1,0:T(2,128)(2,1)S(1)} %reshape.212), channel_id=1, replica_groups=mesh['req'=8,'tp'=4] {'tp'}, dimensions={0}, use_global_device_ids=true | all-gather | bytes 5120 | tf_op jit(solution)/shard_map/all_gather | solution.py:106
  162.0 1.2 convert_bitcast_fusion
  163.4 4.8 %multiply_reduce_fusion.1 = (f32[128]{0:T(128)S(1)}, f32[128,2048]{1,0:T(8,128)S(1)}) fusion(bf16[128,2048]{0,1:T(8,128)(2,1)S(1)} %bitcast.77, bf16[2048,2048]{1,0:T(8,128)(2,1)} %all-gather.6.cloned.1.call-done), kind=kOutput, calls=%fused_computation.27 | convolution fusion | flops 1074265984 | bytes 9961984 | tf_op jit(solution)/shard_map/dot_general | solution.py:111
  168.4 2.5 %multiply_reduce_fusion = (f32[128]{0:T(128)S(1)}, f32[128,2048]{1,0:T(8,128)S(1)}) fusion(bf16[256,2048]{1,0:T(8,128)(2,1)} %all-gather.10.cloned.1.call-done, bf16[512,256]{1,0:T(8,128)(2,1)} %param.25, s32[]{:T(128)S(6)} %select_n.68, bf16[128,2048]{1,0:T(8,128)(2,1)S(1)} %add_convert_fusion.1, bf16[2048,256]{1,0:T(8,128)(2,1)} %all-gather.8.cloned.1.call-done), kind=kOutput, calls=%fused_computation.25 | convolution fusion | flops 269320064 | bytes 3736068 | tf_op jit(solution)/shard_map/dot_general | solution.py:123
  171.2 11.2 %all_to_all.62 = bf16[128,4,512]{2,0,1:T(8,128)(2,1)S(1)} all-to-all(bf16[128,4,512]{2,0,1:T(8,128)(2,1)S(1)} %bitcast.79), channel_id=1, replica_groups=mesh['req'=8,'tp'=4] {'tp'}, dimensions={1} | all-to-all | bytes 1048576 | tf_op jit(solution)/shard_map/all_to_all | solution.py:131
  182.4 0.8 copy.62
  (57 shorter events, 3.1 us)
Async XLA Ops:
  6.5 156.8 %all-gather.6.cloned.1.call-start = ((), (), s32[]{:S(2)}) async-start(), calls=%async_computation.5 | async-start | bytes 10485760 | tf_op jit(solution)/shard_map/all_gather | solution.py:102
  10.4 13.7 %all-to-all-start.1 = ((s32[8,1,6]{2,1,0:T(1,128)}), s32[8,1,6]{2,1,0:T(1,128)S(1)}, u32[]{:S(2)}, u32[]{:S(2)}) async-start(s32[8,1,6]{2,1,0:T(1,128)} %copy.41), calls=%async_computation.1 | async-start | bytes 8192 | tf_op jit(solution)/shard_map/all_to_all | solution.py:73
  26.7 4.6 %copy-start.5 = (s32[1,8]{1,0:T(1,128)S(1)}, s32[1,8]{1,0:T(1,128)}, u32[]{:S(2)}) copy-start(s32[1,8]{1,0:T(1,128)} %param.31) | copy-start | bytes 100
  26.7 4.8 %copy-start.7 = (s32[1,8]{1,0:T(1,128)S(1)}, s32[1,8]{1,0:T(1,128)}, u32[]{:S(2)}) copy-start(s32[1,8]{1,0:T(1,128)} %param.33) | copy-start | bytes 100
  26.7 7.5 %copy-start.6 = (s32[48,1]{0,1:T(1,128)S(1)}, s32[48,1]{0,1:T(1,128)}, u32[]{:S(2)}) copy-start(s32[48,1]{0,1:T(1,128)} %param.29) | copy-start | bytes 580
  26.7 7.7 %copy-start.4 = (s32[1,8]{1,0:T(1,128)S(1)}, s32[1,8]{1,0:T(1,128)}, u32[]{:S(2)}) copy-start(s32[1,8]{1,0:T(1,128)} %param.32) | copy-start | bytes 100
  26.7 73.3 %all-to-all-start.2 = ((bf16[8,6,64,512]{3,2,1,0:T(8,128)(2,1)}), bf16[8,6,64,512]{3,2,1,0:T(8,128)(2,1)S(1)}, u32[]{:S(2)}, u32[]{:S(2)}) async-start(bf16[8,6,64,512]{3,2,1,0:T(8,128)(2,1)} %bitcast.73), calls=%async_computation.2 | async-start | bytes 6291456 | tf_op jit(solution)/shard_map/all_to_all | solution.py:80
  30.5 137.9 %all-gather.10.cloned.1.call-start = ((), (), s32[]{:S(2)}) async-start(), calls=%async_computation.7 | async-start | bytes 1310720 | tf_op jit(solution)/shard_map/all_gather | solution.py:104
  100.0 43.4 %all-to-all-start = ((bf16[4,128,512]{2,1,0:T(8,128)(2,1)}), bf16[4,128,512]{2,1,0:T(8,128)(2,1)}, u32[]{:S(2)}, u32[]{:S(2)}) async-start(bf16[4,128,512]{2,1,0:T(8,128)(2,1)} %bitcast.82), calls=%async_computation | async-start | bytes 1048576 | tf_op jit(solution)/shard_map/all_to_all | solution.py:107
  110.5 8.6 %copy-start = (pred[512,3584]{0,1:T(8,128)(4,1)S(1)}, pred[512,3584]{0,1:T(8,128)(4,1)}, u32[]{:S(2)}) copy-start(pred[512,3584]{0,1:T(8,128)(4,1)} %pad_add_fusion) | copy-start | bytes 5505028
  119.1 16.0 %copy-start.1 = (bf16[3072,256]{0,1:T(8,128)(2,1)S(1)}, bf16[3072,256]{0,1:T(8,128)(2,1)}, u32[]{:S(2)}) copy-start(bf16[3072,256]{0,1:T(8,128)(2,1)} %copy.43) | copy-start | bytes 4718596
  142.4 5.4 %copy-start.2 = (bf16[512]{0:T(512)(128)(2,1)S(1)}, bf16[512]{0:T(512)(128)(2,1)}, u32[]{:S(2)}) copy-start(bf16[512]{0:T(512)(128)(2,1)} %param.24) | copy-start | bytes 3076
  142.4 14.4 %copy-start.3 = (bf16[512]{0:T(512)(128)(2,1)S(1)}, bf16[512]{0:T(512)(128)(2,1)}, u32[]{:S(2)}) copy-start(bf16[512]{0:T(512)(128)(2,1)} %param.28) | copy-start | bytes 3076
  143.4 19.9 %all-to-all-start.3 = ((bf16[4,128,512]{1,2,0:T(8,128)(2,1)}), bf16[4,128,512]{1,2,0:T(8,128)(2,1)S(1)}, u32[]{:S(2)}, u32[]{:S(2)}) async-start(bf16[4,128,512]{1,2,0:T(8,128)(2,1)} %copy.46), calls=%async_computation.3 | async-start | bytes 1048576 | tf_op jit(solution)/shard_map/all_to_all | solution.py:108
  147.1 21.4 %all-gather.8.cloned.1.call-start = ((), (), s32[]{:S(2)}) async-start(), calls=%async_computation.6 | async-start | bytes 1310720 | tf_op jit(solution)/shard_map/all_gather | solution.py:103
Sparse Core Ops, SparseCore 0:
  8.9 60.9 all-gather.5
  71.5 16.7 all-gather.9
  149.5 16.2 all-gather.7
where the time goes:
time: 190 us
  waiting for transfers between devices  66.7 us (35%)
  blocking collectives  25.4 us (13%)
  other arithmetic  25.3 us (13%)
  matrix products  23.1 us (12%)
  starting transfers between devices  19 us (10%)
  local copies, waits for them, and re-layouts  16.9 us (9%)
  between operations  13.4 us (7%)
    all_to_all x1, waiting for transfers between devices, shards(): lax.all_to_all(outgoing, 'req', split_axis=0, concat_axis=0, tiled=True)  61.1 us
    sub x1, other arithmetic, shards(): expo = jnp.exp(scores - highest)  16 us
    all_to_all x1, blocking collectives, shards(): lax.all_to_all(row_out, 'tp', split_axis=1, concat_axis=0, tiled=True)  11.2 us
    all_gather x1, blocking collectives, shards(): full_attn_gain = lax.all_gather(attn_gain, 'tp', axis=0, tiled=True)  8.99 us
    dot_general x1, matrix products, shards(): jnp.einsum('rhd,kd->hrk', query_rows, all_keys, preferred_element_type=jn...  8.55 us
    dot_general x1, matrix products, shards(): jnp.einsum('hrk,kd->rhd', weights, all_values, preferred_element_type=jnp...  7.33 us
    all_to_all x1, starting transfers between devices, shards(): lax.all_to_all(request_table, 'req', split_axis=0, concat_axis=0, tiled=T...  7.28 us
    all_gather x1, blocking collectives, shards(): full_ple_gain = lax.all_gather(ple_gain, 'tp', axis=0, tiled=True)  5.18 us
  transfers between devices with their start and end apart: 7, of which 2 were waited for; matrix products, arithmetic and copies ran while one was open for 32% of the time, Pallas kernels for 0%

commit v1 on v0

--- a/solution.py
+++ b/solution.py
@@ -1,3 +1,4 @@
+import functools
 import math
 import jax
 import jax.numpy as jnp
@@ -6,6 +7,25 @@
 
 D = 2048
 HD = 256
+
+
+def weights_run(tile_in, ax_name):
+    arr_now, res = (lax.axis_size(ax_name), lax.axis_index(ax_name))
+    z2 = list(tile_in.shape)
+    y1 = tile_in.shape[0] // arr_now
+    z2[0] = y1
+    h_now = z2[1]
+    z2[1] = h_now * arr_now
+    block_next = jnp.zeros(z2, tile_in.dtype)
+    for t in range(arr_now):
+        then = lax.dynamic_slice_in_dim(tile_in, (res ^ t) * y1, y1, axis=0)
+        if t:
+            then = lax.ppermute(then, ax_name, [(tick, tick ^ t) for tick in range(arr_now)])
+        block_next = lax.dynamic_update_slice_in_dim(block_next, then, (res ^ t) * h_now, axis=1)
+    return block_next
+
+
+group_frames_on_mesh = functools.partial(weights_run, ax_name="tp")
 
 
 def slot_lookup(positions, counts):
@@ -104,7 +124,7 @@
     full_proj_weight = lax.all_gather(ple_proj_weight, "tp", axis=1, tiled=True)
     full_attn_gain = lax.all_gather(attn_gain, "tp", axis=0, tiled=True)
     full_ple_gain = lax.all_gather(ple_gain, "tp", axis=0, tiled=True)
-    row_hidden = lax.all_to_all(hidden, "tp", split_axis=0, concat_axis=1, tiled=True)
+    row_hidden = group_frames_on_mesh(hidden)
     row_attention = lax.all_to_all(attention, "tp", split_axis=0, concat_axis=1, tiled=True)
     part_rows = row_attention.shape[0]
     row_ple = lax.dynamic_slice_in_dim(ple_input, tp_index * part_rows, part_rows, 0)

time: 190 us -> 197 us (1.037)
  blocking collectives: 25.4 us -> 33.1 us
  waiting for transfers between devices: 66.7 us -> 61.4 us
  local copies, waits for them, and re-layouts: 16.9 us -> 21.6 us
  starting transfers between devices: 19 us -> 16.6 us
    all_gather x1, blocking collectives: 8.99 us -> 16.5 us  [shards(): full_attn_gain = lax.all_gather(attn_gain, 'tp', axis=0, tiled=True)]
    all_to_all x1 -> x0, starting transfers between devices: 4.14 us -> none  [shards(): lax.all_to_all(hidden, 'tp', split_axis=0, concat_axis=1, tiled=True)]
    all_to_all x1, waiting for transfers between devices: 61.1 us -> 57.2 us  [shards(): lax.all_to_all(outgoing, 'req', split_axis=0, concat_axis=0, tiled=True)]
    dynamic_update_slice x0 -> x3, local copies, waits for them, and re-layouts: none -> 2.05 us  [weights_run(): lax.dynamic_update_slice_in_dim(block_next, then, (res ^ t) * h_now, axis=1)]
  transfers between devices with their start and end apart: 7 -> 9, of which waited for: 2 -> 2; matrix products, arithmetic and copies ran while one was open for 32% -> 35% of each run, Pallas kernels for 0% -> 0%
where the time goes in v1:
time: 197 us; the launch traced here: 196 us
  waiting for transfers between devices  61.4 us (31%)
  blocking collectives  33.1 us (17%)
  other arithmetic  27 us (14%)
  matrix products  23.1 us (12%)
  local copies, waits for them, and re-layouts  21.6 us (11%)
  starting transfers between devices  16.6 us (8%)
  between operations  13.5 us (7%)
    all_to_all x1, waiting for transfers between devices, shards(): lax.all_to_all(outgoing, 'req', split_axis=0, concat_axis=0, tiled=True)  57.2 us
    all_gather x1, blocking collectives, shards(): full_attn_gain = lax.all_gather(attn_gain, 'tp', axis=0, tiled=True)  16.5 us
    sub x1, other arithmetic, shards(): expo = jnp.exp(scores - highest)  16 us
    all_to_all x1, blocking collectives, shards(): lax.all_to_all(row_out, 'tp', split_axis=1, concat_axis=0, tiled=True)  11.2 us
    dot_general x1, matrix products, shards(): jnp.einsum('rhd,kd->hrk', query_rows, all_keys, preferred_element_type=jn...  8.55 us
    dot_general x1, matrix products, shards(): jnp.einsum('hrk,kd->rhd', weights, all_values, preferred_element_type=jnp...  7.34 us
    all_to_all x1, starting transfers between devices, shards(): lax.all_to_all(request_table, 'req', split_axis=0, concat_axis=0, tiled=T...  7.28 us
    all_gather x1, blocking collectives, shards(): full_ple_gain = lax.all_gather(ple_gain, 'tp', axis=0, tiled=True)  5.35 us
  transfers between devices with their start and end apart: 9, of which 2 were waited for; matrix products, arithmetic and copies ran while one was open for 35% of the time, Pallas kernels for 0%

profile of v1, /device:TPU:0, one launch (start us, length us, event | category | flops | bytes accessed | tf_op | source)
XLA Modules:
  0.0 196.3 jit_solution(14978938276825330772)
XLA Ops:
  6.5 0.7 all-gather.6.cloned.1.call-update
  7.3 0.9 convert_reduce_fusion.1
  10.4 7.3 %all-to-all-start = ((s32[8,1,6]{2,1,0:T(1,128)}), s32[8,1,6]{2,1,0:T(1,128)S(1)}, u32[]{:S(2)}, u32[]{:S(2)}) async-start(s32[8,1,6]{2,1,0:T(1,128)} %copy.37), calls=%async_computation | async-start | bytes 8192 | tf_op jit(solution)/shard_map/all_to_all | solution.py:93
  17.7 2.7 %constant_dynamic-slice_fusion.2 = (bf16[48,64,256]{2,1,0:T(8,128)(2,1)S(1)}, bf16[48,64,256]{2,1,0:T(8,128)(2,1)S(1)}) fusion(bf16[48,64,512]{2,1,0:T(8,128)(2,1)} %param.22, s32[]{:T(128)S(6)} %select_n.90, bf16[48,64,512]{2,1,0:T(8,128)(2,1)} %param.21), kind=kLoop, calls=%fused_computation.82 | loop fusion | bytes 6291460 | tf_op jit(solution)/shard_map/dynamic_slice | solution.py:96
  20.6 3.4 %all-to-all-done = s32[8,1,6]{2,1,0:T(1,128)S(1)} async-done(((s32[8,1,6]{2,1,0:T(1,128)}), s32[8,1,6]{2,1,0:T(1,128)S(1)}, u32[]{:S(2)}, u32[]{:S(2)}) %all-to-all-start) | async-done | bytes 224 | tf_op jit(solution)/shard_map/all_to_all | solution.py:93
  24.2 2.5 %gather_fusion = bf16[48,64,512]{2,1,0:T(8,128)(2,1)} fusion(bf16[48,64,512]{2,1,0:T(8,128)(2,1)S(1)} %pad_maximum_fusion, s32[1024]{0:T(1024)S(1)} %pad_clamp_fusion.1), kind=kCustom, calls=%fused_computation | custom fusion | bytes 6291648 | tf_op jit(solution)/shard_map/gather | solution.py:99
  26.7 3.8 %all-to-all-start.1 = ((bf16[8,6,64,512]{3,2,1,0:T(8,128)(2,1)}), bf16[8,6,64,512]{3,2,1,0:T(8,128)(2,1)S(1)}, u32[]{:S(2)}, u32[]{:S(2)}) async-start(bf16[8,6,64,512]{3,2,1,0:T(8,128)(2,1)} %bitcast.68), calls=%async_computation.1 | async-start | bytes 6291456 | tf_op jit(solution)/shard_map/all_to_all | solution.py:100
  30.6 0.9 broadcast_in_dim.40
  31.4 1.9 constant_dynamic-slice_fusion.4
  34.2 1.8 constant_dynamic-slice_fusion
  36.0 0.8 copy.47
  38.7 2.4 %compare_and_fusion = pred[512,3072]{0,1:T(8,128)(4,1)S(1)} fusion(s32[512]{0:T(512)S(1)} %broadcast_add_fusion.1, s32[3072]{0:T(1024)S(1)} %broadcast_add_fusion, pred[3072]{0:T(1024)(128)(4,1)S(1)} %fusion.40), kind=kLoop, calls=%fused_computation.12 | loop fusion | flops 3145728 | bytes 1590272 | tf_op jit(solution)/shard_map/and | solution.py:52
  41.1 1.7 pad_add_fusion
  42.7 57.2 %all-to-all-done.1 = bf16[8,6,64,512]{3,2,1,0:T(8,128)(2,1)S(1)} async-done(((bf16[8,6,64,512]{3,2,1,0:T(8,128)(2,1)}), bf16[8,6,64,512]{3,2,1,0:T(8,128)(2,1)S(1)}, u32[]{:S(2)}, u32[]{:S(2)}) %all-to-all-start.1) | async-done | bytes 3145760 | tf_op jit(solution)/shard_map/all_to_all | solution.py:100
  99.9 2.5 %gather_fusion.1 = bf16[48,64,512]{2,1,0:T(8,128)(2,1)} fusion(bf16[48,64,512]{2,1,0:T(8,128)(2,1)S(1)} %bitcast.67, s32[1024]{0:T(1024)S(1)} %pad_clamp_fusion), kind=kCustom, calls=%fused_computation.1 | custom fusion | bytes 6291648 | tf_op jit(solution)/shard_map/gather | solution.py:101
  102.5 2.1 %fusion.52 = (bf16[48,64,256]{2,1,0:T(8,128)(2,1)S(1)}, bf16[48,64,256]{2,1,0:T(8,128)(2,1)S(1)}) fusion(bf16[48,64,512]{2,1,0:T(8,128)(2,1)} %gather_fusion.1), kind=kLoop, calls=%fused_computation.108 | loop fusion | bytes 6291456 | tf_op jit(solution)/shard_map/slice | solution.py:103
  104.6 1.8 copy.39
  106.3 8.6 %fusion.8 = f32[3584,512,2]{1,0,2:T(8,128)} fusion(bf16[512,256]{1,0:T(8,128)(2,1)} %get-tuple-element.22, bf16[3072,256]{1,0:T(8,128)(2,1)S(1)} %bitcast.69, bf16[64,2,8,256]{3,2,1,0:T(8,128)(2,1)} %bitcast.75), kind=kOutput, calls=%fused_computation.18 | convolution fusion | flops 1882718208 | bytes 17039360 | tf_op jit(solution)/shard_map/rhd,kd->hrk/dot_general | solution.py:112
  114.9 16.0 %fusion.53 = (f32[2,512]{1,0:T(2,128)S(1)}, f32[2,512,3584]{1,2,0:T(8,128)}) fusion(f32[3584,512,2]{1,0,2:T(8,128)} %fusion.8, pred[512,3584]{0,1:T(8,128)(4,1)S(1)} %copy-done), kind=kOutput, calls=%fused_computation.109 | output fusion | flops 22023680 | bytes 31199232 | tf_op jit(solution)/shard_map/sub | solution.py:117
  130.9 7.3 %fusion.12 = bf16[512,2,256]{0,2,1:T(8,128)(2,1)S(1)} fusion(f32[2,512,3584]{1,2,0:T(8,128)} %get-tuple-element.16, f32[2,512]{1,0:T(2,128)S(1)} %get-tuple-element.15, bf16[512,256]{0,1:T(8,128)(2,1)} %copy.47, bf16[3072,256]{0,1:T(8,128)(2,1)S(1)} %copy-done.1), kind=kOutput, calls=%fused_computation.22 | convolution fusion | flops 1890320384 | bytes 17043456 | tf_op jit(solution)/shard_map/hrk,kd->rhd/dot_general | solution.py:119
  138.4 0.9 copy.42
  139.3 3.5 %all-to-all-start.2 = ((bf16[4,128,512]{1,2,0:T(8,128)(2,1)}), bf16[4,128,512]{1,2,0:T(8,128)(2,1)S(1)}, u32[]{:S(2)}, u32[]{:S(2)}) async-start(bf16[4,128,512]{1,2,0:T(8,128)(2,1)} %copy.42), calls=%async_computation.2 | async-start | bytes 1048576 | tf_op jit(solution)/shard_map/all_to_all | solution.py:128
  142.8 1.9 collective-permute-start.1
  144.8 16.5 %all-gather = bf16[4,1,512]{2,1,0:T(2,128)(2,1)S(1)} all-gather(bf16[1,1,512]{2,1,0:T(2,128)(2,1)S(1)} %reshape.204), channel_id=1, replica_groups=mesh['req'=8,'tp'=4] {'tp'}, dimensions={0}, use_global_device_ids=true | all-gather | bytes 5120 | tf_op jit(solution)/shard_map/all_gather | solution.py:125
  161.4 5.3 %all-gather.1 = bf16[4,1,512]{2,1,0:T(2,128)(2,1)S(1)} all-gather(bf16[1,1,512]{2,1,0:T(2,128)(2,1)S(1)} %reshape.206), channel_id=1, replica_groups=mesh['req'=8,'tp'=4] {'tp'}, dimensions={0}, use_global_device_ids=true | all-gather | bytes 5120 | tf_op jit(solution)/shard_map/all_gather | solution.py:126
  166.8 0.7 constant_dynamic-update-slice_fusion.2
  168.1 0.7 constant_dynamic-update-slice_fusion
  168.8 4.7 %multiply_reduce_fusion.1 = (f32[128]{0:T(128)S(1)}, f32[128,2048]{1,0:T(8,128)S(1)}) fusion(bf16[128,2048]{0,1:T(8,128)(2,1)S(1)} %bitcast.71, bf16[2048,2048]{1,0:T(8,128)(2,1)} %all-gather.6.cloned.1.call-done), kind=kOutput, calls=%fused_computation.26 | convolution fusion | flops 1074265984 | bytes 9961984 | tf_op jit(solution)/shard_map/dot_general | solution.py:131
  173.6 1.3 add_convert_fusion.1
  174.9 2.5 %multiply_reduce_fusion = (f32[128]{0:T(128)S(1)}, f32[128,2048]{1,0:T(8,128)S(1)}) fusion(bf16[256,2048]{1,0:T(8,128)(2,1)} %all-gather.10.cloned.1.call-done, bf16[512,256]{1,0:T(8,128)(2,1)} %param.25, s32[]{:T(128)S(6)} %select_n.81, bf16[128,2048]{1,0:T(8,128)(2,1)S(1)} %add_convert_fusion.1, bf16[2048,256]{1,0:T(8,128)(2,1)} %all-gather.8.cloned.1.call-done), kind=kOutput, calls=%fused_computation.24 | convolution fusion | flops 269320064 | bytes 3736068 | tf_op jit(solution)/shard_map/dot_general | solution.py:143
  177.7 11.2 %all_to_all.49 = bf16[128,4,512]{2,0,1:T(8,128)(2,1)S(1)} all-to-all(bf16[128,4,512]{2,0,1:T(8,128)(2,1)S(1)} %bitcast.73), channel_id=1, replica_groups=mesh['req'=8,'tp'=4] {'tp'}, dimensions={1} | all-to-all | bytes 1048576 | tf_op jit(solution)/shard_map/all_to_all | solution.py:151
  188.9 0.8 copy.61
  (70 shorter events, 6.6 us)
Async XLA Ops:
  6.5 162.3 %all-gather.6.cloned.1.call-start = ((), (), s32[]{:S(2)}) async-start(), calls=%async_computation.4 | async-start | bytes 10485760 | tf_op jit(solution)/shard_map/all_gather | solution.py:122
  8.2 1.3 copy-start.10
  10.4 13.7 %all-to-all-start = ((s32[8,1,6]{2,1,0:T(1,128)}), s32[8,1,6]{2,1,0:T(1,128)S(1)}, u32[]{:S(2)}, u32[]{:S(2)}) async-start(s32[8,1,6]{2,1,0:T(1,128)} %copy.37), calls=%async_computation | async-start | bytes 8192 | tf_op jit(solution)/shard_map/all_to_all | solution.py:93
  26.7 6.7 %copy-start.7 = (s32[1,8]{1,0:T(1,128)S(1)}, s32[1,8]{1,0:T(1,128)}, u32[]{:S(2)}) copy-start(s32[1,8]{1,0:T(1,128)} %param.31) | copy-start | bytes 100
  26.7 6.9 %copy-start.9 = (s32[1,8]{1,0:T(1,128)S(1)}, s32[1,8]{1,0:T(1,128)}, u32[]{:S(2)}) copy-start(s32[1,8]{1,0:T(1,128)} %param.33) | copy-start | bytes 100
  26.7 73.3 %all-to-all-start.1 = ((bf16[8,6,64,512]{3,2,1,0:T(8,128)(2,1)}), bf16[8,6,64,512]{3,2,1,0:T(8,128)(2,1)S(1)}, u32[]{:S(2)}, u32[]{:S(2)}) async-start(bf16[8,6,64,512]{3,2,1,0:T(8,128)(2,1)} %bitcast.68), calls=%async_computation.1 | async-start | bytes 6291456 | tf_op jit(solution)/shard_map/all_to_all | solution.py:100
  30.5 6.4 %copy-start.8 = (s32[48,1]{0,1:T(1,128)S(1)}, s32[48,1]{0,1:T(1,128)}, u32[]{:S(2)}) copy-start(s32[48,1]{0,1:T(1,128)} %param.29) | copy-start | bytes 580
  30.5 7.7 %copy-start.6 = (s32[1,8]{1,0:T(1,128)S(1)}, s32[1,8]{1,0:T(1,128)}, u32[]{:S(2)}) copy-start(s32[1,8]{1,0:T(1,128)} %param.32) | copy-start | bytes 100
  30.5 144.4 %all-gather.10.cloned.1.call-start = ((), (), s32[]{:S(2)}) async-start(), calls=%async_computation.6 | async-start | bytes 1310720 | tf_op jit(solution)/shard_map/all_gather | solution.py:124
  33.3 133.4 %collective-permute-start = (bf16[128,512]{1,0:T(8,128)(2,1)}, bf16[128,512]{1,0:T(8,128)(2,1)S(1)}, u32[]{:S(2)}, u32[]{:S(2)}) collective-permute-start(bf16[128,512]{1,0:T(8,128)(2,1)} %get-tuple-element.10), channel_id=1, source_target_pairs={{0,1},{1,0},{2,3},{3,2},{4,5},{5,4},{6,7},{7,6},{8,9},{9,8},{10,11... | collective-permute-start | bytes 393224 | tf_op jit(solution)/shard_map/ppermute | solution.py:23
  106.3 8.6 %copy-start = (pred[512,3584]{0,1:T(8,128)(4,1)S(1)}, pred[512,3584]{0,1:T(8,128)(4,1)}, u32[]{:S(2)}) copy-start(pred[512,3584]{0,1:T(8,128)(4,1)} %pad_add_fusion) | copy-start | bytes 5505028
  114.9 16.0 %copy-start.1 = (bf16[3072,256]{0,1:T(8,128)(2,1)S(1)}, bf16[3072,256]{0,1:T(8,128)(2,1)}, u32[]{:S(2)}) copy-start(bf16[3072,256]{0,1:T(8,128)(2,1)} %copy.39) | copy-start | bytes 4718596
  138.2 4.6 %copy-start.3 = (bf16[128,512]{1,0:T(8,128)(2,1)S(1)}, bf16[128,512]{1,0:T(8,128)(2,1)}, u32[]{:S(2)}) copy-start(bf16[128,512]{1,0:T(8,128)(2,1)} %get-tuple-element.12) | copy-start | bytes 393220
  138.2 6.5 %copy-start.2 = (bf16[128,512]{1,0:T(8,128)(2,1)S(1)}, bf16[128,512]{1,0:T(8,128)(2,1)}, u32[]{:S(2)}) copy-start(bf16[128,512]{1,0:T(8,128)(2,1)} %get-tuple-element.9) | copy-start | bytes 393220
  138.2 6.5 %copy-start.4 = (bf16[512]{0:T(512)(128)(2,1)S(1)}, bf16[512]{0:T(512)(128)(2,1)}, u32[]{:S(2)}) copy-start(bf16[512]{0:T(512)(128)(2,1)} %param.24) | copy-start | bytes 3076
  138.2 23.1 %copy-start.5 = (bf16[512]{0:T(512)(128)(2,1)S(1)}, bf16[512]{0:T(512)(128)(2,1)}, u32[]{:S(2)}) copy-start(bf16[512]{0:T(512)(128)(2,1)} %param.28) | copy-start | bytes 3076
  139.3 29.6 %all-to-all-start.2 = ((bf16[4,128,512]{1,2,0:T(8,128)(2,1)}), bf16[4,128,512]{1,2,0:T(8,128)(2,1)S(1)}, u32[]{:S(2)}, u32[]{:S(2)}) async-start(bf16[4,128,512]{1,2,0:T(8,128)(2,1)} %copy.42), calls=%async_computation.2 | async-start | bytes 1048576 | tf_op jit(solution)/shard_map/all_to_all | solution.py:128
  142.7 32.2 %all-gather.8.cloned.1.call-start = ((), (), s32[]{:S(2)}) async-start(), calls=%async_computation.5 | async-start | bytes 1310720 | tf_op jit(solution)/shard_map/all_gather | solution.py:123
  142.8 24.7 %collective-permute-start.1 = (bf16[128,512]{1,0:T(8,128)(2,1)S(1)}, bf16[128,512]{1,0:T(8,128)(2,1)S(1)}, u32[]{:S(2)}, u32[]{:S(2)}) collective-permute-start(bf16[128,512]{1,0:T(8,128)(2,1)S(1)} %copy-done.3), channel_id=1, source_target_pairs={{0,2},{1,3},{2,0},{3,1},{4,6},{5,7},{6,4},{7,5},{8,10},{9,11},{10,... | collective-permute-start | bytes 393224 | tf_op jit(solution)/shard_map/ppermute | solution.py:23
  144.7 23.4 %collective-permute-start.2 = (bf16[128,512]{1,0:T(8,128)(2,1)S(1)}, bf16[128,512]{1,0:T(8,128)(2,1)S(1)}, u32[]{:S(2)}, u32[]{:S(2)}) collective-permute-start(bf16[128,512]{1,0:T(8,128)(2,1)S(1)} %copy-done.2), channel_id=1, source_target_pairs={{0,3},{1,2},{2,1},{3,0},{4,7},{5,6},{6,5},{7,4},{8,11},{9,10},{10,... | collective-permute-start | bytes 393224 | tf_op jit(solution)/shard_map/ppermute | solution.py:23
Sparse Core Ops, SparseCore 0:
  8.9 60.9 all-gather.5
  71.5 16.7 all-gather.9
  145.1 19.1 all-gather.7
